TPU v7x, 512 devices: a whole 4x8x8 slice. The times are simulated.
512 devices in a mesh: wide: 32 (over z, x), narrow: 16 (over y, core).
Axes of the slice: x: 4, y: 8, z: 8, core: 2. Of those that a mesh axis runs over, the one named last changes fastest.
Arguments:
- tokens: bfloat16 [1024, 16384], P('wide', 'narrow'), may hold values from -200 to 200
- norm_gain: float32 [16384], P('narrow'), may hold values from 0.25 to 1.75
- gate_weight: bfloat16 [26624, 16384], P('wide', 'narrow'), may hold values from -0.046875 to 0.046875
- up_weight: bfloat16 [26624, 16384], P('wide', 'narrow'), may hold values from -0.046875 to 0.046875
- down_weight: bfloat16 [26624, 16384], P('wide', 'narrow'), may hold values from -0.0390625 to 0.0390625
Outputs:
- ffn_out: bfloat16 [1024, 16384], P('wide', 'narrow')
All inputs are finite; a program needn't handle non-finite values.
Results may differ from a plain program's by a relative error of at most 0.03.
Values may be sent and summed in bfloat16 or wider, within the bound.
No kernel may reach another device: no remote copies, remote signals or barrier semaphores. Data moves between devices by JAX's collectives and lax.ppermute only.
A program may use at most 64 MiB of HBM per device.

v0:
```python
import jax
import jax.numpy as jnp
from jax import lax
from jax.sharding import Mesh, PartitionSpec as P

EPS = 1e-05
NARROW = ("y", "core")


def local(tokens, norm_gain, gate_weight, up_weight, down_weight):
    width = gate_weight.shape[0]
    n_z = lax.axis_size("z")
    n_x = lax.axis_size("x")
    n_narrow = lax.axis_size(NARROW)
    model_width = tokens.shape[1] * n_narrow
    rows = tokens.shape[0]
    spread = jnp.broadcast_to(tokens[None], (n_z,) + tokens.shape)
    near = lax.all_to_all(spread, "z", 0, 0)
    spread = jnp.broadcast_to(near[:, None], (n_z, n_x) + tokens.shape)
    whole = lax.all_to_all(spread, "x", 1, 1).reshape(n_z * n_x * rows, tokens.shape[1])
    values = whole.astype(jnp.float32)
    partial = jnp.sum(values * values, axis=1)
    scaled = (values * norm_gain).astype(jnp.bfloat16)
    dims = (((1,), (1,)), ((), ()))
    joined = jnp.concatenate([gate_weight, up_weight], axis=0)
    pair = lax.dot_general(scaled, joined, dims, preferred_element_type=jnp.float32).astype(
        jnp.bfloat16
    )
    n_y = lax.axis_size("y")
    n_c = lax.axis_size("core")
    step = pair.shape[0] // (n_y * n_c)
    pieces = pair.reshape(n_y, n_c, step, pair.shape[1])
    inner = jnp.sum(lax.all_to_all(pieces, "core", 1, 1).astype(jnp.float32), axis=1).astype(
        jnp.bfloat16
    )
    part = jnp.sum(lax.all_to_all(inner, "y", 0, 0).astype(jnp.float32), axis=0)
    shares = partial.reshape(n_y, n_c, step)
    shares = jnp.sum(lax.all_to_all(shares, "core", 1, 1), axis=1)
    mine_sq = jnp.sum(lax.all_to_all(shares, "y", 0, 0), axis=0)
    scale = lax.rsqrt(mine_sq / model_width + EPS)[:, None]
    sums = part.astype(jnp.float32)
    mine = (jax.nn.silu(sums[:, :width] * scale) * (sums[:, width:] * scale)).astype(jnp.bfloat16)
    half = width // 2
    first = lax.all_gather(mine[:, :half], NARROW, axis=0, tiled=True)
    second = lax.all_gather(mine[:, half:], NARROW, axis=0, tiled=True)
    down = (
        jnp.dot(first, down_weight[:half], preferred_element_type=jnp.float32)
        + jnp.dot(second, down_weight[half:], preferred_element_type=jnp.float32)
    ).astype(jnp.bfloat16)
    pieces = down.reshape(n_z, n_x, rows, down.shape[1])
    across = jnp.sum(lax.all_to_all(pieces, "x", 1, 1).astype(jnp.float32), axis=1).astype(
        jnp.bfloat16
    )
    return jnp.sum(lax.all_to_all(across, "z", 0, 0).astype(jnp.float32), axis=0).astype(
        jnp.bfloat16
    )


def solution(mesh):
    n_wide, n_narrow = mesh.devices.shape
    n_x = len({device.coords[0] for device in mesh.devices[:, 0]})
    view = Mesh(mesh.devices.reshape(n_wide // n_x, n_x, n_narrow // 2, 2), ("z", "x", "y", "core"))
    wide = ("z", "x")
    in_specs = (P(wide, NARROW), P(NARROW), P(wide, NARROW), P(wide, NARROW), P(wide, NARROW))
    out_specs = P(wide, NARROW)
    return jax.shard_map(local, mesh=view, in_specs=in_specs, out_specs=out_specs, check_vma=False)
```

profile of v0, /device:TPU:2, one launch (start us, length us, event | category | flops | bytes accessed | tf_op | source)
XLA Modules:
  0.0 226.4 jit_solution(4716993163845403259)
XLA Ops:
  0.0 0.9 broadcast_in_dim.4
  0.9 27.6 %all_to_all.44 = bf16[8,32,1024]{2,1,0:T(8,128)(2,1)S(1)} all-to-all(bf16[8,32,1024]{2,1,0:T(8,128)(2,1)S(1)} %broadcast_in_dim.4), channel_id=1, replica_groups=mesh['z'=8,'x'=4,'y'=8,'core'=2] {'z'}, dimensions={0} | all-to-all | bytes 1048576 | tf_op jit(solution)/shard_map/all_to_all | solution.py:18
  28.5 0.3 broadcast_in_dim.5
  28.8 27.7 %all_to_all.45 = bf16[8,4,32,1024]{3,2,0,1:T(8,128)(2,1)S(1)} all-to-all(bf16[8,4,32,1024]{3,2,0,1:T(8,128)(2,1)S(1)} %broadcast_in_dim.5), channel_id=1, replica_groups=mesh['z'=8,'x'=4,'y'=8,'core'=2] {'x'}, dimensions={1} | all-to-all | bytes 4194304 | tf_op jit(solution)/shard_map/all_to_all | solution.py:20
  56.5 0.5 multiply_reduce_fusion
  57.1 3.7 %all_to_all.46 = f32[2,1,512]{2,1,0:T(1,128)S(1)} all-to-all(f32[2,1,512]{2,1,0:T(1,128)S(1)} %reshape.28), channel_id=1, replica_groups=mesh['z'=8,'x'=4,'y'=8,'core'=2] {'core'}, dimensions={0} | all-to-all | bytes 8192 | tf_op jit(solution)/shard_map/all_to_all | solution.py:38
  60.8 0.5 broadcast.14
  61.3 0.7 reduce.5
  62.1 0.6 bitcast_reduce_fusion
  62.7 0.5 copy_convert_fusion
  63.2 0.2 copy-done.1
  63.4 0.6 fusion
  64.0 0.8 copy-done.2
  64.8 0.5 copy-done.3
  65.3 4.2 %convolution_convert_fusion = bf16[1024,1664]{1,0:T(8,128)(2,1)S(1)} fusion(bf16[1024,1024]{1,0:T(8,128)(2,1)S(1)} %fusion, bf16[832,1024]{1,0:T(8,128)(2,1)S(1)} %copy-done.2, bf16[832,1024]{1,0:T(8,128)(2,1)S(1)} %copy-done.3), kind=kOutput, calls=%fused_computation.4 | convolution fusion | flops 3498180608 | bytes 8912896 | tf_op jit(solution)/shard_map/dot_general | solution.py:26
  69.6 0.3 copy.13
  69.8 6.5 %all_to_all.47 = bf16[8,2,64,1664]{3,2,0,1:T(8,128)(2,1)S(1)} all-to-all(bf16[8,2,64,1664]{3,2,0,1:T(8,128)(2,1)S(1)} %copy.13), channel_id=1, replica_groups=mesh['z'=8,'x'=4,'y'=8,'core'=2] {'core'}, dimensions={1} | all-to-all | bytes 6815744 | tf_op jit(solution)/shard_map/all_to_all | solution.py:33
  76.3 7.1 %all-to-all-start.5 = ((f32[8,1,64]{2,1,0:T(1,128)}), f32[8,1,64]{2,1,0:T(1,128)S(1)}, u32[]{:S(2)}, u32[]{:S(2)}) async-start(f32[8,1,64]{2,1,0:T(1,128)} %bitcast.2), calls=%async_computation.5 | async-start | bytes 8192 | tf_op jit(solution)/shard_map/all_to_all | solution.py:39
  83.4 2.3 %reduce_sum.72 = bf16[8,64,1664]{2,1,0:T(8,128)(2,1)} reduce(bf16[8,2,64,1664]{3,2,0,1:T(8,128)(2,1)S(1)} %all_to_all.47, bf16[]{:T(256)} %constant.9.clone.1), dimensions={1}, to_apply=%region_0.0 | reduce | flops 851968 | bytes 5111810 | tf_op jit(solution)/shard_map/reduce_sum | solution.py:33
  85.7 5.3 %all-to-all-done.5 = f32[8,1,64]{2,1,0:T(1,128)S(1)} async-done(((f32[8,1,64]{2,1,0:T(1,128)}), f32[8,1,64]{2,1,0:T(1,128)S(1)}, u32[]{:S(2)}, u32[]{:S(2)}) %all-to-all-start.5) | async-done | bytes 2080 | tf_op jit(solution)/shard_map/all_to_all | solution.py:39
  91.0 3.6 %all-to-all-start.3 = ((bf16[8,64,1664]{2,1,0:T(8,128)(2,1)}), bf16[8,64,1664]{2,1,0:T(8,128)(2,1)S(1)}, u32[]{:S(2)}, u32[]{:S(2)}) async-start(bf16[8,64,1664]{2,1,0:T(8,128)(2,1)} %reduce_sum.72), calls=%async_computation.3 | async-start | bytes 3407872 | tf_op jit(solution)/shard_map/all_to_all | solution.py:36
  94.7 41.8 %all-to-all-done.3 = bf16[8,64,1664]{2,1,0:T(8,128)(2,1)S(1)} async-done(((bf16[8,64,1664]{2,1,0:T(8,128)(2,1)}), bf16[8,64,1664]{2,1,0:T(8,128)(2,1)S(1)}, u32[]{:S(2)}, u32[]{:S(2)}) %all-to-all-start.3) | async-done | bytes 1703968 | tf_op jit(solution)/shard_map/all_to_all | solution.py:36
  136.5 0.2 convert_reduce_fusion
  137.0 17.6 %all_gather.7 = bf16[1024,416]{1,0:T(8,128)(2,1)S(1)} all-gather(bf16[64,416]{1,0:T(8,128)(2,1)S(1)} %get-tuple-element.5), channel_id=1, replica_groups=mesh['z'=8,'x'=4,'y'=8,'core'=2] {'y','core'}, dimensions={0}, use_global_device_ids=true | all-gather | bytes 905216 | tf_op jit(solution)/shard_map/all_gather | solution.py:45
  154.6 18.6 %all_gather.6 = bf16[1024,416]{1,0:T(8,128)(2,1)S(1)} all-gather(bf16[64,416]{1,0:T(8,128)(2,1)S(1)} %get-tuple-element.6), channel_id=1, replica_groups=mesh['z'=8,'x'=4,'y'=8,'core'=2] {'y','core'}, dimensions={0}, use_global_device_ids=true | all-gather | bytes 905216 | tf_op jit(solution)/shard_map/all_gather | solution.py:44
  173.2 1.3 fusion.5
  174.5 1.3 add_convert_fusion
  175.8 0.3 copy.15
  176.1 29.6 %all_to_all.48 = bf16[8,4,32,1024]{3,2,0,1:T(8,128)(2,1)S(1)} all-to-all(bf16[8,4,32,1024]{3,2,0,1:T(8,128)(2,1)S(1)} %copy.15), channel_id=1, replica_groups=mesh['z'=8,'x'=4,'y'=8,'core'=2] {'x'}, dimensions={1} | all-to-all | bytes 4194304 | tf_op jit(solution)/shard_map/all_to_all | solution.py:51
  205.7 0.4 reduce_sum.77
  206.1 19.7 %all_to_all.49 = bf16[8,32,1024]{2,1,0:T(8,128)(2,1)S(1)} all-to-all(bf16[8,32,1024]{2,1,0:T(8,128)(2,1)S(1)} %reduce_sum.77), channel_id=1, replica_groups=mesh['z'=8,'x'=4,'y'=8,'core'=2] {'z'}, dimensions={0} | all-to-all | bytes 1048576 | tf_op jit(solution)/shard_map/all_to_all | solution.py:54
  225.7 0.7 reduce_sum.78
  (13 shorter events, 0.5 us)
Async XLA Ops:
  62.7 0.7 copy-start.1
  63.4 1.5 copy-start.2
  63.4 2.0 copy-start.3
  76.3 14.7 %all-to-all-start.5 = ((f32[8,1,64]{2,1,0:T(1,128)}), f32[8,1,64]{2,1,0:T(1,128)S(1)}, u32[]{:S(2)}, u32[]{:S(2)}) async-start(f32[8,1,64]{2,1,0:T(1,128)} %bitcast.2), calls=%async_computation.5 | async-start | bytes 8192 | tf_op jit(solution)/shard_map/all_to_all | solution.py:39
  91.0 45.5 %all-to-all-start.3 = ((bf16[8,64,1664]{2,1,0:T(8,128)(2,1)}), bf16[8,64,1664]{2,1,0:T(8,128)(2,1)S(1)}, u32[]{:S(2)}, u32[]{:S(2)}) async-start(bf16[8,64,1664]{2,1,0:T(8,128)(2,1)} %reduce_sum.72), calls=%async_computation.3 | async-start | bytes 3407872 | tf_op jit(solution)/shard_map/all_to_all | solution.py:36
  94.7 78.6 %copy-start = (bf16[832,1024]{1,0:T(8,128)(2,1)S(1)}, bf16[832,1024]{1,0:T(8,128)(2,1)}, u32[]{:S(2)}) copy-start(bf16[832,1024]{1,0:T(8,128)(2,1)} %param.9) | copy-start | bytes 5111812
where the time goes:
time: 227 us; the launch traced here: 226 us
  blocking collectives  151 us (67%)
  waiting for transfers between devices  47.2 us (21%)
  starting transfers between devices  10.7 us (5%)
  matrix products  6.75 us (3%)
  other arithmetic  6.62 us (3%)
  local copies, waits for them, and re-layouts  4.1 us (2%)
    all_to_all x1, waiting for transfers between devices, local(): part = jnp.sum(lax.all_to_all(inner, 'y', 0, 0).astype(jnp.float32), axis=0)  41.8 us
    all_to_all x1, blocking collectives, local(): lax.all_to_all(pieces, 'x', 1, 1).astype(jnp.float32)  29.6 us
    all_to_all x1, blocking collectives, local(): lax.all_to_all(spread, 'x', 1, 1).reshape(n_z * n_x * rows, tokens.shape[1])  27.7 us
    all_to_all x1, blocking collectives, local(): near = lax.all_to_all(spread, 'z', 0, 0)  27.6 us
    all_to_all x1, blocking collectives, local(): lax.all_to_all(across, 'z', 0, 0).astype(jnp.float32)  19.7 us
    all_gather x1, blocking collectives, local(): first = lax.all_gather(mine[:, :half], NARROW, axis=0, tiled=True)  18.6 us
    all_gather x1, blocking collectives, local(): second = lax.all_gather(mine[:, half:], NARROW, axis=0, tiled=True)  17.6 us
    all_to_all x1, starting transfers between devices, local(): mine_sq = jnp.sum(lax.all_to_all(shares, 'y', 0, 0), axis=0)  7.1 us
  transfers between devices with their start and end apart: 2, of which 2 were waited for; matrix products, arithmetic and copies ran while one was open for 1% of the time, Pallas kernels for 0%

commit v1 on v0

--- a/solution.py
+++ b/solution.py
@@ -42,7 +42,11 @@
     mine = (jax.nn.silu(sums[:, :width] * scale) * (sums[:, width:] * scale)).astype(jnp.bfloat16)
     half = width // 2
     first = lax.all_gather(mine[:, :half], NARROW, axis=0, tiled=True)
-    second = lax.all_gather(mine[:, half:], NARROW, axis=0, tiled=True)
+    own = mine[:, half:]
+    size = lax.axis_size(NARROW)
+    blocks = jnp.stack([own for _ in range(size)])
+    blocks = lax.all_to_all(blocks, NARROW, split_axis=0, concat_axis=0)
+    second = jnp.concatenate(blocks, axis=0)
     down = (
         jnp.dot(first, down_weight[:half], preferred_element_type=jnp.float32)
         + jnp.dot(second, down_weight[half:], preferred_element_type=jnp.float32)

time: 227 us -> 240 us (1.057)
  matrix products: 6.75 us -> 10.9 us
  blocking collectives: 151 us -> 155 us
  starting transfers between devices: 10.7 us -> 14.3 us
    all_gather x1, blocking collectives: 18.6 us -> 40.5 us  [local(): first = lax.all_gather(mine[:, :half], NARROW, axis=0, tiled=True)]
    all_gather x1 -> x0, blocking collectives: 17.6 us -> none  [local(): second = lax.all_gather(mine[:, half:], NARROW, axis=0, tiled=True)]
    all_to_all x0 -> x1, starting transfers between devices: none -> 3.65 us  [local(): blocks = lax.all_to_all(blocks, NARROW, split_axis=0, concat_axis=0)]
  transfers between devices with their start and end apart: 2 -> 3, of which waited for: 2 -> 2; matrix products, arithmetic and copies ran while one was open for 1% -> 2% of each run, Pallas kernels for 0% -> 0%
where the time goes in v1:
time: 240 us
  blocking collectives  155 us (65%)
  waiting for transfers between devices  47.2 us (20%)
  starting transfers between devices  14.3 us (6%)
  matrix products  10.9 us (5%)
  other arithmetic  6.62 us (3%)
  local copies, waits for them, and re-layouts  5.18 us (2%)
    all_to_all x1, waiting for transfers between devices, local(): part = jnp.sum(lax.all_to_all(inner, 'y', 0, 0).astype(jnp.float32), axis=0)  41.8 us
    all_gather x1, blocking collectives, local(): first = lax.all_gather(mine[:, :half], NARROW, axis=0, tiled=True)  40.5 us
    all_to_all x1, blocking collectives, local(): lax.all_to_all(pieces, 'x', 1, 1).astype(jnp.float32)  29.6 us
    all_to_all x1, blocking collectives, local(): lax.all_to_all(spread, 'x', 1, 1).reshape(n_z * n_x * rows, tokens.shape[1])  27.7 us
    all_to_all x1, blocking collectives, local(): near = lax.all_to_all(spread, 'z', 0, 0)  27.6 us
    all_to_all x1, blocking collectives, local(): lax.all_to_all(across, 'z', 0, 0).astype(jnp.float32)  19.7 us
    all_to_all x1, starting transfers between devices, local(): mine_sq = jnp.sum(lax.all_to_all(shares, 'y', 0, 0), axis=0)  7.1 us
    all_to_all x1, blocking collectives, local(): lax.all_to_all(pieces, 'core', 1, 1).astype(jnp.float32)  6.47 us
  transfers between devices with their start and end apart: 3, of which 2 were waited for; matrix products, arithmetic and copies ran while one was open for 2% of the time, Pallas kernels for 0%

profile of v1, /device:TPU:2, one launch (start us, length us, event | category | flops | bytes accessed | tf_op | source)
XLA Modules:
  0.0 239.5 jit_solution(8470520324391888589)
XLA Ops:
  0.0 0.9 broadcast_in_dim.4
  0.9 27.6 %all_to_all.49 = bf16[8,32,1024]{2,1,0:T(8,128)(2,1)S(1)} all-to-all(bf16[8,32,1024]{2,1,0:T(8,128)(2,1)S(1)} %broadcast_in_dim.4), channel_id=1, replica_groups=mesh['z'=8,'x'=4,'y'=8,'core'=2] {'z'}, dimensions={0} | all-to-all | bytes 1048576 | tf_op jit(solution)/shard_map/all_to_all | solution.py:18
  28.5 0.3 broadcast_in_dim.5
  28.8 27.7 %all_to_all.50 = bf16[8,4,32,1024]{3,2,0,1:T(8,128)(2,1)S(1)} all-to-all(bf16[8,4,32,1024]{3,2,0,1:T(8,128)(2,1)S(1)} %broadcast_in_dim.5), channel_id=1, replica_groups=mesh['z'=8,'x'=4,'y'=8,'core'=2] {'x'}, dimensions={1} | all-to-all | bytes 4194304 | tf_op jit(solution)/shard_map/all_to_all | solution.py:20
  56.5 0.5 multiply_reduce_fusion
  57.1 3.7 %all_to_all.51 = f32[2,1,512]{2,1,0:T(1,128)S(1)} all-to-all(f32[2,1,512]{2,1,0:T(1,128)S(1)} %reshape.34), channel_id=1, replica_groups=mesh['z'=8,'x'=4,'y'=8,'core'=2] {'core'}, dimensions={0} | all-to-all | bytes 8192 | tf_op jit(solution)/shard_map/all_to_all | solution.py:38
  60.8 0.5 broadcast.16
  61.3 0.7 reduce.5
  62.1 0.6 bitcast_reduce_fusion
  62.7 0.5 copy_convert_fusion
  63.4 0.6 fusion
  64.0 0.8 copy-done.2
  64.8 0.5 copy-done.3
  65.3 4.2 %convolution_convert_fusion = bf16[1024,1664]{1,0:T(8,128)(2,1)S(1)} fusion(bf16[1024,1024]{1,0:T(8,128)(2,1)S(1)} %fusion, bf16[832,1024]{1,0:T(8,128)(2,1)S(1)} %copy-done.2, bf16[832,1024]{1,0:T(8,128)(2,1)S(1)} %copy-done.3), kind=kOutput, calls=%fused_computation.4 | convolution fusion | flops 3498180608 | bytes 8912896 | tf_op jit(solution)/shard_map/dot_general | solution.py:26
  69.6 0.3 copy.13
  69.8 6.5 %all_to_all.52 = bf16[8,2,64,1664]{3,2,0,1:T(8,128)(2,1)S(1)} all-to-all(bf16[8,2,64,1664]{3,2,0,1:T(8,128)(2,1)S(1)} %copy.13), channel_id=1, replica_groups=mesh['z'=8,'x'=4,'y'=8,'core'=2] {'core'}, dimensions={1} | all-to-all | bytes 6815744 | tf_op jit(solution)/shard_map/all_to_all | solution.py:33
  76.3 7.1 %all-to-all-start.5 = ((f32[8,1,64]{2,1,0:T(1,128)}), f32[8,1,64]{2,1,0:T(1,128)S(1)}, u32[]{:S(2)}, u32[]{:S(2)}) async-start(f32[8,1,64]{2,1,0:T(1,128)} %bitcast.2), calls=%async_computation.5 | async-start | bytes 8192 | tf_op jit(solution)/shard_map/all_to_all | solution.py:39
  83.4 2.3 reduce_sum.72
  85.7 5.3 %all-to-all-done.5 = f32[8,1,64]{2,1,0:T(1,128)S(1)} async-done(((f32[8,1,64]{2,1,0:T(1,128)}), f32[8,1,64]{2,1,0:T(1,128)S(1)}, u32[]{:S(2)}, u32[]{:S(2)}) %all-to-all-start.5) | async-done | bytes 2080 | tf_op jit(solution)/shard_map/all_to_all | solution.py:39
  91.0 3.6 %all-to-all-start.3 = ((bf16[8,64,1664]{2,1,0:T(8,128)(2,1)}), bf16[8,64,1664]{2,1,0:T(8,128)(2,1)S(1)}, u32[]{:S(2)}, u32[]{:S(2)}) async-start(bf16[8,64,1664]{2,1,0:T(8,128)(2,1)} %reduce_sum.72), calls=%async_computation.3 | async-start | bytes 3407872 | tf_op jit(solution)/shard_map/all_to_all | solution.py:36
  94.7 41.8 %all-to-all-done.3 = bf16[8,64,1664]{2,1,0:T(8,128)(2,1)S(1)} async-done(((bf16[8,64,1664]{2,1,0:T(8,128)(2,1)}), bf16[8,64,1664]{2,1,0:T(8,128)(2,1)S(1)}, u32[]{:S(2)}, u32[]{:S(2)}) %all-to-all-start.3) | async-done | bytes 1703968 | tf_op jit(solution)/shard_map/all_to_all | solution.py:36
  136.5 0.2 convert_reduce_fusion
  137.0 1.1 stack.2
  138.1 3.7 %all-to-all-start.6 = ((bf16[16,64,416]{2,1,0:T(8,128)(2,1)}), bf16[16,64,416]{2,1,0:T(8,128)(2,1)S(1)}, u32[]{:S(2)}, u32[]{:S(2)}) async-start(bf16[16,64,416]{2,1,0:T(8,128)(2,1)} %stack.2), calls=%async_computation.6 | async-start | bytes 2097152 | tf_op jit(solution)/shard_map/all_to_all | solution.py:48
  141.7 40.5 %all_gather.3 = bf16[1024,416]{1,0:T(8,128)(2,1)S(1)} all-gather(bf16[64,416]{1,0:T(8,128)(2,1)S(1)} %get-tuple-element.6), channel_id=1, replica_groups=mesh['z'=8,'x'=4,'y'=8,'core'=2] {'y','core'}, dimensions={0}, use_global_device_ids=true | all-gather | bytes 905216 | tf_op jit(solution)/shard_map/all_gather | solution.py:44
  182.2 3.2 %fusion.5 = f32[1024,1024]{1,0:T(8,128)} fusion(bf16[1024,416]{1,0:T(8,128)(2,1)S(1)} %all_gather.3, bf16[832,1024]{1,0:T(8,128)(2,1)S(1)} %copy-done), kind=kOutput, calls=%fused_computation.11 | convolution fusion | flops 872415232 | bytes 6094848 | tf_op jit(solution)/shard_map/dot_general | solution.py:51
  185.4 3.4 %add_convert_fusion = bf16[1024,1024]{1,0:T(8,128)(2,1)S(1)} fusion(f32[1024,1024]{1,0:T(8,128)} %fusion.5, bf16[1024,416]{1,0:T(8,128)(2,1)S(1)} %bitcast.17, bf16[832,1024]{1,0:T(8,128)(2,1)S(1)} %copy-done), kind=kOutput, calls=%fused_computation.2 | convolution fusion | flops 874512384 | bytes 8192000 | tf_op jit(solution)/shard_map/dot_general | solution.py:52
  188.9 0.3 copy.15
  189.1 29.6 %all_to_all.53 = bf16[8,4,32,1024]{3,2,0,1:T(8,128)(2,1)S(1)} all-to-all(bf16[8,4,32,1024]{3,2,0,1:T(8,128)(2,1)S(1)} %copy.15), channel_id=1, replica_groups=mesh['z'=8,'x'=4,'y'=8,'core'=2] {'x'}, dimensions={1} | all-to-all | bytes 4194304 | tf_op jit(solution)/shard_map/all_to_all | solution.py:55
  218.7 0.4 reduce_sum.77
  219.2 19.7 %all_to_all.54 = bf16[8,32,1024]{2,1,0:T(8,128)(2,1)S(1)} all-to-all(bf16[8,32,1024]{2,1,0:T(8,128)(2,1)S(1)} %reduce_sum.77), channel_id=1, replica_groups=mesh['z'=8,'x'=4,'y'=8,'core'=2] {'z'}, dimensions={0} | all-to-all | bytes 1048576 | tf_op jit(solution)/shard_map/all_to_all | solution.py:58
  238.8 0.7 reduce_sum.78
  (15 shorter events, 0.7 us)
Async XLA Ops:
  62.7 0.7 copy-start.1
  63.4 1.5 copy-start.2
  63.4 2.0 copy-start.3
  76.3 14.7 %all-to-all-start.5 = ((f32[8,1,64]{2,1,0:T(1,128)}), f32[8,1,64]{2,1,0:T(1,128)S(1)}, u32[]{:S(2)}, u32[]{:S(2)}) async-start(f32[8,1,64]{2,1,0:T(1,128)} %bitcast.2), calls=%async_computation.5 | async-start | bytes 8192 | tf_op jit(solution)/shard_map/all_to_all | solution.py:39
  91.0 45.5 %all-to-all-start.3 = ((bf16[8,64,1664]{2,1,0:T(8,128)(2,1)}), bf16[8,64,1664]{2,1,0:T(8,128)(2,1)S(1)}, u32[]{:S(2)}, u32[]{:S(2)}) async-start(bf16[8,64,1664]{2,1,0:T(8,128)(2,1)} %reduce_sum.72), calls=%async_computation.3 | async-start | bytes 3407872 | tf_op jit(solution)/shard_map/all_to_all | solution.py:36
  137.0 45.3 %copy-start = (bf16[832,1024]{1,0:T(8,128)(2,1)S(1)}, bf16[832,1024]{1,0:T(8,128)(2,1)}, u32[]{:S(2)}) copy-start(bf16[832,1024]{1,0:T(8,128)(2,1)} %param.9) | copy-start | bytes 5111812
  138.1 47.4 %all-to-all-start.6 = ((bf16[16,64,416]{2,1,0:T(8,128)(2,1)}), bf16[16,64,416]{2,1,0:T(8,128)(2,1)S(1)}, u32[]{:S(2)}, u32[]{:S(2)}) async-start(bf16[16,64,416]{2,1,0:T(8,128)(2,1)} %stack.2), calls=%async_computation.6 | async-start | bytes 2097152 | tf_op jit(solution)/shard_map/all_to_all | solution.py:48
